TPU v7x, 128 devices: a whole 4x4x4 slice. The times are simulated.
128 devices in a mesh: row: 8 (over z_hi, x), col: 16 (over z_lo, y, core).
Axes of the slice: x: 4, y: 4, z: 4 (z_hi: 2, z_lo: 2; z = z_hi * 2 + z_lo), core: 2. Of those that a mesh axis runs over, the one named last changes fastest.
Arguments:
- tokens: bfloat16 [1024, 8192], P(('row', 'col')), may hold values from -6 to 6
- gain: float32 [8192], replicated, may hold values from 0.5 to 1.5
- grad_out: bfloat16 [1024, 8192], P(('row', 'col')), may hold values from -4 to 4
- pre_gate: bfloat16 [1024, 28672], P('col', 'row'), may hold values from -6 to 6
- pre_up: bfloat16 [1024, 28672], P('col', 'row'), may hold values from -6 to 6
- gate_weight: bfloat16 [8192, 28672], P('col', 'row'), may hold values from -0.0625 to 0.0625
- up_weight: bfloat16 [8192, 28672], P('col', 'row'), may hold values from -0.0625 to 0.0625
- down_weight: bfloat16 [28672, 8192], P('row', 'col'), may hold values from -0.03125 to 0.03125
Outputs:
- grad_tokens: bfloat16 [1024, 8192], P(('row', 'col'))
- grad_gain: float32 [8192], replicated
- grad_gate: bfloat16 [8192, 28672], P('col', 'row')
- grad_up: bfloat16 [8192, 28672], P('col', 'row')
- grad_down: bfloat16 [28672, 8192], P('row', 'col')
All inputs are finite; a program needn't handle non-finite values.
Results may differ from a plain program's by a relative error of at most 0.0057.
Values may be sent and summed in bfloat16 or wider, within the bound.
No kernel may reach another device: no remote copies, remote signals or barrier semaphores. Data moves between devices by JAX's collectives and lax.ppermute only.
A program may use at most 192 MiB of HBM per device.

v0:
```python
import jax
import jax.numpy as jnp
from jax import lax
from jax.sharding import PartitionSpec as P

epsilon = 1e-05


def swiglu_grads(hidden_grad, pre_gate, pre_up):
    gate_wide = pre_gate.astype(jnp.float32)
    up_wide = pre_up.astype(jnp.float32)
    sigmoid = jax.nn.sigmoid(gate_wide)
    silu = gate_wide * sigmoid
    hidden = (silu * up_wide).astype(jnp.bfloat16)
    up_grad = (hidden_grad * silu).astype(jnp.bfloat16)
    gate_grad = (hidden_grad * up_wide * sigmoid * (1.0 + gate_wide * (1.0 - sigmoid))).astype(
        jnp.bfloat16
    )
    return (hidden, gate_grad, up_grad)


def local(tokens, gain, grad_out, pre_gate, pre_up, gate_weight, up_weight, down_weight):
    tokens_wide = tokens.astype(jnp.float32)
    inverse_rms = lax.rsqrt(jnp.mean(tokens_wide * tokens_wide, axis=1, keepdims=True) + epsilon)
    normed = tokens_wide * inverse_rms
    scaled = (normed * gain).astype(jnp.bfloat16)
    grid_input, grid_grad = (
        lax.all_to_all(scaled, "col", split_axis=1, concat_axis=0, tiled=True),
        lax.all_to_all(grad_out, "col", split_axis=1, concat_axis=0, tiled=True),
    )
    all_input, all_grad = (
        lax.all_gather(grid_input, "row", axis=0, tiled=True),
        lax.all_gather(grid_grad, "row", axis=0, tiled=True),
    )
    partial_grad = jnp.einsum(
        "td,fd->tf", all_grad, down_weight, preferred_element_type=jnp.float32
    )
    summed_grad = lax.psum(partial_grad, "col")
    hidden_piece, gate_piece, up_piece = swiglu_grads(
        summed_grad,
        lax.all_gather(pre_gate, "col", axis=0, tiled=True),
        lax.all_gather(pre_up, "col", axis=0, tiled=True),
    )
    down_total = jnp.einsum("tf,td->fd", hidden_piece, all_grad, preferred_element_type=jnp.float32)
    gate_total = jnp.einsum("td,tf->df", all_input, gate_piece, preferred_element_type=jnp.float32)
    up_total = jnp.einsum("td,tf->df", all_input, up_piece, preferred_element_type=jnp.float32)
    new_rows = jnp.einsum("tf,df->td", gate_piece, gate_weight, preferred_element_type=jnp.float32)
    new_rows = new_rows + jnp.einsum(
        "tf,df->td", up_piece, up_weight, preferred_element_type=jnp.float32
    )
    back_rows = new_rows
    results = (down_total, gate_total, up_total, back_rows)
    down_total, gate_total, up_total, back_rows = results
    grid_back = lax.psum_scatter(back_rows, "row", scatter_dimension=0, tiled=True)
    normed_grad = lax.all_to_all(grid_back, "col", split_axis=0, concat_axis=1, tiled=True)
    grad_gain = lax.psum(jnp.sum(normed_grad * normed, axis=0), ("row", "col"))
    scaled_grad = normed_grad * gain
    inner = jnp.mean(scaled_grad * normed, axis=1, keepdims=True)
    grad_tokens = (
        grad_out.astype(jnp.float32) + inverse_rms * (scaled_grad - normed * inner)
    ).astype(jnp.bfloat16)
    return (
        grad_tokens,
        grad_gain,
        gate_total.astype(jnp.bfloat16),
        up_total.astype(jnp.bfloat16),
        down_total.astype(jnp.bfloat16),
    )


def solution(mesh):
    in_specs = (
        P(("row", "col"), None),
        P(),
        P(("row", "col"), None),
        P("col", "row"),
        P("col", "row"),
        P("col", "row"),
        P("col", "row"),
        P("row", "col"),
    )
    out_specs = (P(("row", "col"), None), P(), P("col", "row"), P("col", "row"), P("row", "col"))
    return jax.shard_map(local, mesh=mesh, in_specs=in_specs, out_specs=out_specs, check_vma=False)
```

profile of v0, /device:TPU:1, one launch (start us, length us, event | category | flops | bytes accessed | tf_op | source)
XLA Modules:
  0.0 565.8 jit_solution(3937982184247556598)
XLA Ops:
  7.2 0.0 all-gather.5.cloned.1.call-start
  7.2 13.5 %all_to_all.57 = bf16[8,16,512]{2,0,1:T(8,128)(2,1)} all-to-all(bf16[8,16,512]{2,0,1:T(8,128)(2,1)} %bitcast.27), channel_id=1, replica_groups=mesh['row'=8,'col'=16] {'col'}, dimensions={1} | all-to-all | bytes 262144 | tf_op jit(solution)/shard_map/all_to_all | solution.py:29
  20.7 0.0 all-gather.5.cloned.1.call-update
  20.7 0.0 all-gather.7.cloned.1.call-start
  20.8 0.7 all-gather.7.cloned.1.call-update
  21.5 0.0 all-gather.9.cloned.1.call-start
  21.5 0.7 all-gather.9.cloned.1.call-update
  22.2 0.0 all-reduce.2.cloned.1.call-start
  22.3 43.9 %all-gather.5.cloned.1.call-done = bf16[1024,512]{1,0:T(8,128)(2,1)} async-done(((bf16[128,512]{1,0:T(8,128)(2,1)}), bf16[1024,512]{1,0:T(8,128)(2,1)}) %all-gather.5.cloned.1.call-update) | async-done | bytes 1048592 | tf_op jit(solution)/shard_map/all_gather | solution.py:33
  66.2 11.5 %fusion.26 = f32[1024,3584]{1,0:T(8,128)} fusion(bf16[1024,512]{1,0:T(8,128)(2,1)} %all-gather.5.cloned.1.call-done, bf16[3584,512]{1,0:T(8,128)(2,1)} %param.15), kind=kOutput, calls=%fused_computation.36 | convolution fusion | flops 3758096384 | bytes 19398656 | tf_op jit(solution)/shard_map/td,fd->tf/dot_general | solution.py:35
  77.7 0.0 all-reduce.2.cloned.1.call-update
  77.7 0.0 reduce-scatter.2.cloned.1.call-start
  77.8 38.1 %all-gather.7.cloned.1.call-done = bf16[1024,3584]{1,0:T(8,128)(2,1)} async-done(((bf16[64,3584]{1,0:T(8,128)(2,1)}), bf16[1024,3584]{1,0:T(8,128)(2,1)}) %all-gather.7.cloned.1.call-update) | async-done | bytes 7340048 | tf_op jit(solution)/shard_map/all_gather | solution.py:42
  115.8 49.7 %all-gather.9.cloned.1.call-done = bf16[1024,3584]{1,0:T(8,128)(2,1)} async-done(((bf16[64,3584]{1,0:T(8,128)(2,1)}), bf16[1024,3584]{1,0:T(8,128)(2,1)}) %all-gather.9.cloned.1.call-update) | async-done | bytes 7340048 | tf_op jit(solution)/shard_map/all_gather | solution.py:41
  165.6 177.7 %all-reduce.2.cloned.1.call-done = f32[1024,3584]{1,0:T(8,128)} async-done(((f32[1024,3584]{1,0:T(8,128)}), f32[1024,3584]{1,0:T(8,128)}) %all-reduce.2.cloned.1.call-update) | async-done | bytes 14680080 | tf_op jit(solution)/shard_map/psum | solution.py:38
  343.3 0.0 copy-start.6
  343.3 12.5 %multiply_convert_fusion = (bf16[1024,3584]{1,0:T(8,128)(2,1)S(1)}, bf16[1024,3584]{1,0:T(8,128)(2,1)S(1)}) fusion(f32[1024,3584]{1,0:T(8,128)} %all-reduce.2.cloned.1.call-done, bf16[1024,3584]{1,0:T(8,128)(2,1)} %all-gather.9.cloned.1.call-done, bf16[1024,3584]{1,0:T(8,128)(2,1)} %all-gather.7.cloned.1.call-done), kind=kLoop, calls=%fused_computation.13 | loop fusion | flops 55050240 | bytes 44040192 | tf_op jit(solution)/shard_map/convert_element_type | solution.py:15
  355.8 0.0 copy-start
  355.8 0.0 copy-start.1
  355.8 0.0 copy-done.6
  355.8 0.0 copy-start.7
  355.8 4.0 fusion.27
  359.8 0.0 copy-done
  359.8 2.0 copy-done.1
  361.8 0.0 copy-done.7
  361.8 0.0 copy-start.2
  361.8 0.0 copy-start.5
  361.8 0.0 copy-start.8
  361.8 5.3 convolution_add_fusion
  367.1 0.0 reduce-scatter.2.cloned.1.call-update
  367.1 75.7 %reduce-scatter.2.cloned.1.call-done = f32[128,512]{1,0:T(8,128)} async-done(((f32[1024,512]{1,0:T(8,128)}), f32[128,512]{1,0:T(8,128)}) %reduce-scatter.2.cloned.1.call-update) | async-done | bytes 262160 | tf_op jit(solution)/shard_map/reduce_scatter | solution.py:54
  442.8 6.5 %all-to-all-start.1 = ((f32[16,8,512]{2,1,0:T(8,128)}), f32[16,8,512]{2,1,0:T(8,128)S(1)}, u32[]{:S(2)}, u32[]{:S(2)}) async-start(f32[16,8,512]{2,1,0:T(8,128)} %bitcast.28), calls=%async_computation.2 | async-start | bytes 524288 | tf_op jit(solution)/shard_map/all_to_all | solution.py:55
  449.3 0.0 copy-done.2
  449.3 0.2 fusion.24
  449.5 7.0 %all-to-all-done.1 = f32[16,8,512]{2,1,0:T(8,128)S(1)} async-done(((f32[16,8,512]{2,1,0:T(8,128)}), f32[16,8,512]{2,1,0:T(8,128)S(1)}, u32[]{:S(2)}, u32[]{:S(2)}) %all-to-all-start.1) | async-done | bytes 262176 | tf_op jit(solution)/shard_map/all_to_all | solution.py:55
  456.5 0.0 copy-done.5
  456.5 0.9 fusion.22
  457.5 4.0 all-to-all-start.2
  461.5 0.0 copy-start.4
  461.5 0.2 all-gather.11.cloned.1.call-start
  461.8 0.0 copy-done.8
  461.8 10.3 %fusion.10 = bf16[3584,512]{1,0:T(8,128)(2,1)} fusion(bf16[1024,512]{1,0:T(8,128)(2,1)S(1)} %copy-done.8, bf16[1024,3584]{1,0:T(8,128)(2,1)} %all-gather.7.cloned.1.call-done, bf16[1024,3584]{1,0:T(8,128)(2,1)} %all-gather.9.cloned.1.call-done), kind=kOutput, calls=%fused_computation.15 | convolution fusion | flops 3789291520 | bytes 19398656 | tf_op jit(solution)/shard_map/tf,td->fd/dot_general | solution.py:44
  472.1 0.0 all-to-all-done.2
  472.1 0.0 copy-start.3
  472.1 0.7 copy-done.3
  472.7 0.0 all-gather.11.cloned.1.call-update
  472.8 67.5 %psum.15 = f32[8192]{0:T(1024)} all-reduce(f32[8192]{0:T(1024)S(1)} %get-tuple-element.5), channel_id=1, replica_groups=mesh['row'=8,'col'=16] {'row','col'}, use_global_device_ids=true, to_apply=%region_5.0 | all-reduce | flops 8192 | bytes 65536 | tf_op jit(solution)/shard_map/psum | solution.py:56
  540.3 0.0 copy-done.4
  540.3 0.8 fusion.21
  541.1 0.0 all-gather.11.cloned.1.call-done
  541.1 0.0 copy-start.9
  541.1 9.3 %convolution_convert_fusion = bf16[512,3584]{1,0:T(8,128)(2,1)} fusion(bf16[1024,512]{1,0:T(8,128)(2,1)} %all-gather.11.cloned.1.call-done, bf16[1024,3584]{1,0:T(8,128)(2,1)} %copy-done.1), kind=kOutput, calls=%fused_computation.16 | convolution fusion | flops 3759931392 | bytes 12058624 | tf_op jit(solution)/shard_map/td,tf->df/dot_general | solution.py:46
  550.4 0.0 copy-done.9
  550.4 8.5 %convolution_convert_fusion.1 = bf16[512,3584]{1,0:T(8,128)(2,1)} fusion(bf16[1024,512]{1,0:T(8,128)(2,1)S(1)} %copy-done.9, bf16[1024,3584]{1,0:T(8,128)(2,1)} %copy-done), kind=kOutput, calls=%fused_computation.17 | convolution fusion | flops 3759931392 | bytes 12058624 | tf_op jit(solution)/shard_map/td,tf->df/dot_general | solution.py:45
  (2 shorter events, 0.0 us)
Async XLA Ops:
  7.2 59.0 %all-gather.5.cloned.1.call-start = ((), (), s32[]{:S(2)}) async-start(), calls=%async_computation.4 | async-start | bytes 1179648 | tf_op jit(solution)/shard_map/all_gather | solution.py:33
  20.7 95.1 %all-gather.7.cloned.1.call-start = ((), (), s32[]{:S(2)}) async-start(), calls=%async_computation.6 | async-start | bytes 7798784 | tf_op jit(solution)/shard_map/all_gather | solution.py:42
  21.5 144.1 %all-gather.9.cloned.1.call-start = ((), (), s32[]{:S(2)}) async-start(), calls=%async_computation.7 | async-start | bytes 7798784 | tf_op jit(solution)/shard_map/all_gather | solution.py:41
  22.2 321.1 %all-reduce.2.cloned.1.call-start = ((), (), s32[]{:S(2)}) async-start(), calls=%async_computation.5 | async-start | bytes 29360128 | tf_op jit(solution)/shard_map/psum | solution.py:38
  77.7 365.1 %reduce-scatter.2.cloned.1.call-start = ((), (), s32[]{:S(2)}) async-start(), calls=%async_computation.8 | async-start | bytes 2359296 | tf_op jit(solution)/shard_map/reduce_scatter | solution.py:54
  343.3 12.5 %copy-start.6 = (bf16[512,3584]{1,0:T(8,128)(2,1)S(1)}, bf16[512,3584]{1,0:T(8,128)(2,1)}, u32[]{:S(2)}) copy-start(bf16[512,3584]{1,0:T(8,128)(2,1)} %param.13) | copy-start | bytes 11010052
  355.8 4.0 copy-start
  355.8 6.0 %copy-start.1 = (bf16[1024,3584]{1,0:T(8,128)(2,1)}, bf16[1024,3584]{1,0:T(8,128)(2,1)S(1)}, u32[]{:S(2)}) copy-start(bf16[1024,3584]{1,0:T(8,128)(2,1)S(1)} %get-tuple-element.7) | copy-start | bytes 22020100
  355.8 6.0 %copy-start.7 = (bf16[512,3584]{1,0:T(8,128)(2,1)S(1)}, bf16[512,3584]{1,0:T(8,128)(2,1)}, u32[]{:S(2)}) copy-start(bf16[512,3584]{1,0:T(8,128)(2,1)} %param.14) | copy-start | bytes 11010052
  361.8 87.6 %copy-start.2 = (bf16[8,8192]{1,0:T(8,128)(2,1)S(1)}, bf16[8,8192]{1,0:T(8,128)(2,1)}, u32[]{:S(2)}) copy-start(bf16[8,8192]{1,0:T(8,128)(2,1)} %param.8) | copy-start | bytes 393220
  361.8 94.8 %copy-start.5 = (f32[8192]{0:T(1024)S(1)}, f32[8192]{0:T(1024)}, u32[]{:S(2)}) copy-start(f32[8192]{0:T(1024)} %param.9) | copy-start | bytes 98308
  361.8 100.0 %copy-start.8 = (bf16[1024,512]{1,0:T(8,128)(2,1)S(1)}, bf16[1024,512]{1,0:T(8,128)(2,1)}, u32[]{:S(2)}) copy-start(bf16[1024,512]{1,0:T(8,128)(2,1)} %all-gather.5.cloned.1.call-done) | copy-start | bytes 3145732
  442.8 13.7 %all-to-all-start.1 = ((f32[16,8,512]{2,1,0:T(8,128)}), f32[16,8,512]{2,1,0:T(8,128)S(1)}, u32[]{:S(2)}, u32[]{:S(2)}) async-start(f32[16,8,512]{2,1,0:T(8,128)} %bitcast.28), calls=%async_computation.2 | async-start | bytes 524288 | tf_op jit(solution)/shard_map/all_to_all | solution.py:55
  457.5 14.6 %all-to-all-start.2 = ((bf16[8,16,512]{2,0,1:T(8,128)(2,1)}), bf16[8,16,512]{2,0,1:T(8,128)(2,1)S(1)}, u32[]{:S(2)}, u32[]{:S(2)}) async-start(bf16[8,16,512]{2,0,1:T(8,128)(2,1)} %bitcast.7), calls=%async_computation.3 | async-start | bytes 262144 | tf_op jit(solution)/shard_map/all_to_all | solution.py:28
  461.5 78.8 %copy-start.4 = (bf16[8,8192]{1,0:T(8,128)(2,1)S(1)}, bf16[8,8192]{1,0:T(8,128)(2,1)}, u32[]{:S(2)}) copy-start(bf16[8,8192]{1,0:T(8,128)(2,1)} %param.10) | copy-start | bytes 393220
  461.5 79.6 %all-gather.11.cloned.1.call-start = ((), (), s32[]{:S(2)}) async-start(), calls=%async_computation.9 | async-start | bytes 1179648 | tf_op jit(solution)/shard_map/all_gather | solution.py:32
  472.1 0.7 copy-start.3
  541.1 9.3 %copy-start.9 = (bf16[1024,512]{1,0:T(8,128)(2,1)S(1)}, bf16[1024,512]{1,0:T(8,128)(2,1)}, u32[]{:S(2)}) copy-start(bf16[1024,512]{1,0:T(8,128)(2,1)} %all-gather.11.cloned.1.call-done) | copy-start | bytes 3145732
Sparse Core Ops, SparseCore 0:
  20.8 45.2 all-gather.4
  67.9 47.9 all-gather.6
  117.5 47.9 all-gather.8
  168.0 175.2 all-reduce.1
  367.2 75.5 reduce-scatter.1
  472.9 45.2 all-gather.10
where the time goes:
time: 566 us
  waiting for transfers between devices  394 us (70%)
  blocking collectives  81 us (14%)
  matrix products  48.9 us (9%)
  other arithmetic  14.4 us (3%)
  between operations  14.2 us (3%)
  starting transfers between devices  11 us (2%)
    psum x1, waiting for transfers between devices, local(): summed_grad = lax.psum(partial_grad, 'col')  178 us
    reduce_scatter x1, waiting for transfers between devices, local(): lax.psum_scatter(back_rows, 'row', scatter_dimension=0, tiled=True)  75.7 us
    psum x1, blocking collectives, local(): grad_gain = lax.psum(jnp.sum(normed_grad * normed, axis=0), ('row', 'col'))  67.5 us
    all_gather x1, waiting for transfers between devices, local(): lax.all_gather(pre_gate, 'col', axis=0, tiled=True)  49.7 us
    all_gather x1, waiting for transfers between devices, local(): lax.all_gather(grid_grad, 'row', axis=0, tiled=True)  43.9 us
    all_gather x1, waiting for transfers between devices, local(): lax.all_gather(pre_up, 'col', axis=0, tiled=True)  38.1 us
    all_to_all x1, blocking collectives, local(): lax.all_to_all(grad_out, 'col', split_axis=1, concat_axis=0, tiled=True)  13.5 us
    convert_element_type x1, other arithmetic, swiglu_grads(): up_grad = (hidden_grad * silu).astype(jnp.bfloat16)  12.5 us
  transfers between devices with their start and end apart: 8, of which 6 were waited for; matrix products, arithmetic and copies ran while one was open for 4% of the time, Pallas kernels for 0%

commit v1 on v0

--- a/solution.py
+++ b/solution.py
@@ -39,7 +39,9 @@
     hidden_piece, gate_piece, up_piece = swiglu_grads(
         summed_grad,
         lax.all_gather(pre_gate, "col", axis=0, tiled=True),
-        lax.all_gather(pre_up, "col", axis=0, tiled=True),
+        jnp.concatenate(
+            lax.all_to_all(jnp.stack([pre_up] * lax.axis_size("col")), "col", 0, 0), axis=0
+        ),
     )
     down_total = jnp.einsum("tf,td->fd", hidden_piece, all_grad, preferred_element_type=jnp.float32)
     gate_total = jnp.einsum("td,tf->df", all_input, gate_piece, preferred_element_type=jnp.float32)

time: 566 us -> 594 us (1.049)
  blocking collectives: 81 us -> 195 us
  waiting for transfers between devices: 394 us -> 306 us
    all_to_all x0 -> x1, blocking collectives: none -> 114 us  [local(): lax.all_to_all(jnp.stack([pre_up] * lax.axis_size('col')), 'col', 0, 0)]
    all_gather x1, waiting for transfers between devices: 49.7 us -> 0.01 us  [local(): lax.all_gather(pre_gate, 'col', axis=0, tiled=True)]
    all_gather x1 -> x0, waiting for transfers between devices: 38.1 us -> none  [local(): lax.all_gather(pre_up, 'col', axis=0, tiled=True)]
  transfers between devices with their start and end apart: 8 -> 7, of which waited for: 6 -> 4; matrix products, arithmetic and copies ran while one was open for 4% -> 4% of each run, Pallas kernels for 0% -> 0%
where the time goes in v1:
time: 594 us
  waiting for transfers between devices  306 us (52%)
  blocking collectives  195 us (33%)
  matrix products  49 us (8%)
  other arithmetic  14.4 us (2%)
  between operations  13.9 us (2%)
  starting transfers between devices  10.9 us (2%)
    psum x1, waiting for transfers between devices, local(): summed_grad = lax.psum(partial_grad, 'col')  178 us
    all_to_all x1, blocking collectives, local(): lax.all_to_all(jnp.stack([pre_up] * lax.axis_size('col')), 'col', 0, 0)  114 us
    reduce_scatter x1, waiting for transfers between devices, local(): lax.psum_scatter(back_rows, 'row', scatter_dimension=0, tiled=True)  75.7 us
    psum x1, blocking collectives, local(): grad_gain = lax.psum(jnp.sum(normed_grad * normed, axis=0), ('row', 'col'))  67.4 us
    all_gather x1, waiting for transfers between devices, local(): lax.all_gather(grid_grad, 'row', axis=0, tiled=True)  44.7 us
    all_to_all x1, blocking collectives, local(): lax.all_to_all(grad_out, 'col', split_axis=1, concat_axis=0, tiled=True)  13.5 us
    convert_element_type x1, other arithmetic, swiglu_grads(): up_grad = (hidden_grad * silu).astype(jnp.bfloat16)  12.5 us
  transfers between devices with their start and end apart: 7, of which 4 were waited for; matrix products, arithmetic and copies ran while one was open for 4% of the time, Pallas kernels for 0%

profile of v1, /device:TPU:1, one launch (start us, length us, event | category | flops | bytes accessed | tf_op | source)
XLA Modules:
  0.0 593.7 jit_solution(18030427107382117201)
XLA Ops:
  7.2 0.0 all-gather.4.cloned.1.call-start
  7.2 13.5 %all_to_all.62 = bf16[8,16,512]{2,0,1:T(8,128)(2,1)} all-to-all(bf16[8,16,512]{2,0,1:T(8,128)(2,1)} %bitcast.31), channel_id=1, replica_groups=mesh['row'=8,'col'=16] {'col'}, dimensions={1} | all-to-all | bytes 262144 | tf_op jit(solution)/shard_map/all_to_all | solution.py:29
  20.7 0.0 all-gather.4.cloned.1.call-update
  20.7 0.0 all-gather.6.cloned.1.call-start
  20.8 0.7 all-gather.6.cloned.1.call-update
  21.5 0.0 all-reduce.2.cloned.1.call-start
  21.5 44.7 %all-gather.4.cloned.1.call-done = bf16[1024,512]{1,0:T(8,128)(2,1)} async-done(((bf16[128,512]{1,0:T(8,128)(2,1)}), bf16[1024,512]{1,0:T(8,128)(2,1)}) %all-gather.4.cloned.1.call-update) | async-done | bytes 1048592 | tf_op jit(solution)/shard_map/all_gather | solution.py:33
  66.2 11.5 %fusion.26 = f32[1024,3584]{1,0:T(8,128)} fusion(bf16[1024,512]{1,0:T(8,128)(2,1)} %all-gather.4.cloned.1.call-done, bf16[3584,512]{1,0:T(8,128)(2,1)} %param.15), kind=kOutput, calls=%fused_computation.36 | convolution fusion | flops 3758096384 | bytes 19398656 | tf_op jit(solution)/shard_map/td,fd->tf/dot_general | solution.py:35
  77.7 0.0 copy-start.5
  77.7 0.0 all-reduce.2.cloned.1.call-update
  77.7 0.0 reduce-scatter.2.cloned.1.call-start
  77.8 0.9 copy-done.5
  78.7 0.7 stack.2
  79.4 114.0 %all_to_all.63 = bf16[16,64,3584]{2,1,0:T(8,128)(2,1)} all-to-all(bf16[16,64,3584]{2,1,0:T(8,128)(2,1)S(1)} %stack.2), channel_id=1, replica_groups=mesh['row'=8,'col'=16] {'col'}, dimensions={0} | all-to-all | bytes 14680064 | tf_op jit(solution)/shard_map/all_to_all | solution.py:43
  193.4 0.0 all-gather.6.cloned.1.call-done
  193.4 178.1 %all-reduce.2.cloned.1.call-done = f32[1024,3584]{1,0:T(8,128)} async-done(((f32[1024,3584]{1,0:T(8,128)}), f32[1024,3584]{1,0:T(8,128)}) %all-reduce.2.cloned.1.call-update) | async-done | bytes 14680080 | tf_op jit(solution)/shard_map/psum | solution.py:38
  371.6 0.0 copy-start.7
  371.6 12.5 %multiply_convert_fusion = (bf16[1024,3584]{1,0:T(8,128)(2,1)S(1)}, bf16[1024,3584]{1,0:T(8,128)(2,1)S(1)}) fusion(f32[1024,3584]{1,0:T(8,128)} %all-reduce.2.cloned.1.call-done, bf16[1024,3584]{1,0:T(8,128)(2,1)} %all-gather.6.cloned.1.call-done, bf16[16,64,3584]{2,1,0:T(8,128)(2,1)} %all_to_all.63), kind=kLoop, calls=%fused_computation.13 | loop fusion | flops 55050240 | bytes 44040192 | tf_op jit(solution)/shard_map/convert_element_type | solution.py:15
  384.1 0.0 copy-start
  384.1 0.0 copy-start.1
  384.1 0.0 copy-done.7
  384.1 0.0 copy-start.8
  384.1 4.0 fusion.27
  388.1 0.0 copy-done
  388.1 2.0 copy-done.1
  390.1 0.0 copy-done.8
  390.1 0.0 copy-start.2
  390.1 0.0 copy-start.6
  390.1 0.0 copy-start.9
  390.1 5.3 convolution_add_fusion
  395.4 0.0 reduce-scatter.2.cloned.1.call-update
  395.4 75.7 %reduce-scatter.2.cloned.1.call-done = f32[128,512]{1,0:T(8,128)} async-done(((f32[1024,512]{1,0:T(8,128)}), f32[128,512]{1,0:T(8,128)}) %reduce-scatter.2.cloned.1.call-update) | async-done | bytes 262160 | tf_op jit(solution)/shard_map/reduce_scatter | solution.py:56
  471.1 6.5 %all-to-all-start.2 = ((f32[16,8,512]{2,1,0:T(8,128)}), f32[16,8,512]{2,1,0:T(8,128)S(1)}, u32[]{:S(2)}, u32[]{:S(2)}) async-start(f32[16,8,512]{2,1,0:T(8,128)} %bitcast.32), calls=%async_computation.3 | async-start | bytes 524288 | tf_op jit(solution)/shard_map/all_to_all | solution.py:57
  477.6 0.0 copy-done.2
  477.6 0.2 fusion.24
  477.8 7.0 %all-to-all-done.2 = f32[16,8,512]{2,1,0:T(8,128)S(1)} async-done(((f32[16,8,512]{2,1,0:T(8,128)}), f32[16,8,512]{2,1,0:T(8,128)S(1)}, u32[]{:S(2)}, u32[]{:S(2)}) %all-to-all-start.2) | async-done | bytes 262176 | tf_op jit(solution)/shard_map/all_to_all | solution.py:57
  484.8 0.0 copy-done.6
  484.8 0.9 fusion.22
  485.7 4.0 all-to-all-start.3
  489.8 0.2 all-gather.8.cloned.1.call-start
  490.0 0.0 copy-done.9
  490.0 0.0 copy-start.4
  490.0 10.3 %fusion.10 = bf16[3584,512]{1,0:T(8,128)(2,1)} fusion(bf16[1024,512]{1,0:T(8,128)(2,1)S(1)} %copy-done.9, bf16[1024,3584]{1,0:T(8,128)(2,1)} %bitcast.26, bf16[1024,3584]{1,0:T(8,128)(2,1)} %all-gather.6.cloned.1.call-done), kind=kOutput, calls=%fused_computation.15 | convolution fusion | flops 3789291520 | bytes 19398656 | tf_op jit(solution)/shard_map/tf,td->fd/dot_general | solution.py:46
  500.4 0.0 all-to-all-done.3
  500.4 0.0 copy-start.3
  500.4 0.7 copy-done.3
  501.0 0.0 all-gather.8.cloned.1.call-update
  501.1 67.4 %psum.15 = f32[8192]{0:T(1024)} all-reduce(f32[8192]{0:T(1024)S(1)} %get-tuple-element.5), channel_id=1, replica_groups=mesh['row'=8,'col'=16] {'row','col'}, use_global_device_ids=true, to_apply=%region_5.0 | all-reduce | flops 8192 | bytes 65536 | tf_op jit(solution)/shard_map/psum | solution.py:58
  568.5 0.0 copy-done.4
  568.5 0.8 fusion.21
  569.3 0.0 all-gather.8.cloned.1.call-done
  569.3 0.0 copy-start.10
  569.3 9.3 %convolution_convert_fusion = bf16[512,3584]{1,0:T(8,128)(2,1)} fusion(bf16[1024,512]{1,0:T(8,128)(2,1)} %all-gather.8.cloned.1.call-done, bf16[1024,3584]{1,0:T(8,128)(2,1)} %copy-done.1), kind=kOutput, calls=%fused_computation.16 | convolution fusion | flops 3759931392 | bytes 12058624 | tf_op jit(solution)/shard_map/td,tf->df/dot_general | solution.py:48
  578.6 0.0 copy-done.10
  578.6 8.5 %convolution_convert_fusion.1 = bf16[512,3584]{1,0:T(8,128)(2,1)} fusion(bf16[1024,512]{1,0:T(8,128)(2,1)S(1)} %copy-done.10, bf16[1024,3584]{1,0:T(8,128)(2,1)} %copy-done), kind=kOutput, calls=%fused_computation.17 | convolution fusion | flops 3759931392 | bytes 12058624 | tf_op jit(solution)/shard_map/td,tf->df/dot_general | solution.py:47
  (2 shorter events, 0.0 us)
Async XLA Ops:
  7.2 59.0 %all-gather.4.cloned.1.call-start = ((), (), s32[]{:S(2)}) async-start(), calls=%async_computation.5 | async-start | bytes 1179648 | tf_op jit(solution)/shard_map/all_gather | solution.py:33
  20.7 172.7 %all-gather.6.cloned.1.call-start = ((), (), s32[]{:S(2)}) async-start(), calls=%async_computation.7 | async-start | bytes 7798784 | tf_op jit(solution)/shard_map/all_gather | solution.py:41
  21.5 350.1 %all-reduce.2.cloned.1.call-start = ((), (), s32[]{:S(2)}) async-start(), calls=%async_computation.6 | async-start | bytes 29360128 | tf_op jit(solution)/shard_map/psum | solution.py:38
  77.7 1.0 copy-start.5
  77.7 393.4 %reduce-scatter.2.cloned.1.call-start = ((), (), s32[]{:S(2)}) async-start(), calls=%async_computation.8 | async-start | bytes 2359296 | tf_op jit(solution)/shard_map/reduce_scatter | solution.py:56
  371.6 12.5 %copy-start.7 = (bf16[512,3584]{1,0:T(8,128)(2,1)S(1)}, bf16[512,3584]{1,0:T(8,128)(2,1)}, u32[]{:S(2)}) copy-start(bf16[512,3584]{1,0:T(8,128)(2,1)} %param.13) | copy-start | bytes 11010052
  384.1 4.0 copy-start
  384.1 6.0 %copy-start.1 = (bf16[1024,3584]{1,0:T(8,128)(2,1)}, bf16[1024,3584]{1,0:T(8,128)(2,1)S(1)}, u32[]{:S(2)}) copy-start(bf16[1024,3584]{1,0:T(8,128)(2,1)S(1)} %get-tuple-element.7) | copy-start | bytes 22020100
  384.1 6.0 %copy-start.8 = (bf16[512,3584]{1,0:T(8,128)(2,1)S(1)}, bf16[512,3584]{1,0:T(8,128)(2,1)}, u32[]{:S(2)}) copy-start(bf16[512,3584]{1,0:T(8,128)(2,1)} %param.14) | copy-start | bytes 11010052
  390.1 87.6 %copy-start.2 = (bf16[8,8192]{1,0:T(8,128)(2,1)S(1)}, bf16[8,8192]{1,0:T(8,128)(2,1)}, u32[]{:S(2)}) copy-start(bf16[8,8192]{1,0:T(8,128)(2,1)} %param.8) | copy-start | bytes 393220
  390.1 94.8 %copy-start.6 = (f32[8192]{0:T(1024)S(1)}, f32[8192]{0:T(1024)}, u32[]{:S(2)}) copy-start(f32[8192]{0:T(1024)} %param.9) | copy-start | bytes 98308
  390.1 100.0 %copy-start.9 = (bf16[1024,512]{1,0:T(8,128)(2,1)S(1)}, bf16[1024,512]{1,0:T(8,128)(2,1)}, u32[]{:S(2)}) copy-start(bf16[1024,512]{1,0:T(8,128)(2,1)} %all-gather.4.cloned.1.call-done) | copy-start | bytes 3145732
  471.1 13.7 %all-to-all-start.2 = ((f32[16,8,512]{2,1,0:T(8,128)}), f32[16,8,512]{2,1,0:T(8,128)S(1)}, u32[]{:S(2)}, u32[]{:S(2)}) async-start(f32[16,8,512]{2,1,0:T(8,128)} %bitcast.32), calls=%async_computation.3 | async-start | bytes 524288 | tf_op jit(solution)/shard_map/all_to_all | solution.py:57
  485.7 14.6 %all-to-all-start.3 = ((bf16[8,16,512]{2,0,1:T(8,128)(2,1)}), bf16[8,16,512]{2,0,1:T(8,128)(2,1)S(1)}, u32[]{:S(2)}, u32[]{:S(2)}) async-start(bf16[8,16,512]{2,0,1:T(8,128)(2,1)} %bitcast.8), calls=%async_computation.4 | async-start | bytes 262144 | tf_op jit(solution)/shard_map/all_to_all | solution.py:28
  489.8 79.5 %all-gather.8.cloned.1.call-start = ((), (), s32[]{:S(2)}) async-start(), calls=%async_computation.9 | async-start | bytes 1179648 | tf_op jit(solution)/shard_map/all_gather | solution.py:32
  490.0 78.5 %copy-start.4 = (bf16[8,8192]{1,0:T(8,128)(2,1)S(1)}, bf16[8,8192]{1,0:T(8,128)(2,1)}, u32[]{:S(2)}) copy-start(bf16[8,8192]{1,0:T(8,128)(2,1)} %param.10) | copy-start | bytes 393220
  500.4 0.7 copy-start.3
  569.3 9.3 %copy-start.10 = (bf16[1024,512]{1,0:T(8,128)(2,1)S(1)}, bf16[1024,512]{1,0:T(8,128)(2,1)}, u32[]{:S(2)}) copy-start(bf16[1024,512]{1,0:T(8,128)(2,1)} %all-gather.8.cloned.1.call-done) | copy-start | bytes 3145732
Sparse Core Ops, SparseCore 0:
  20.8 45.2 all-gather.3
  67.9 125.1 all-gather.5
  195.6 175.9 all-reduce.1
  395.5 75.5 reduce-scatter.1
  501.2 45.1 all-gather.7
